TPU v7x, 512 devices: a whole 4x4x16 slice. The times are simulated.
512 devices in a mesh: blk: 32 (over z, core), col: 16 (over y, x).
Axes of the slice: x: 4, y: 4, z: 16, core: 2. Of those that a mesh axis runs over, the one named last changes fastest.
Arguments:
- density: float32 [96, 7, 256, 256], P('blk', None, 'col'), as said below
- band_widths: int32 [96], P('blk'), may hold values from 1 to 3, as said below
Outputs:
- purified: float32 [96, 7, 256, 256], P('blk', None, 'col')
Inputs may be any that keep to these rules, and one draw needn't show every extreme that they name: `band_widths`: each block row keeps between 1 and 3 blocks on each side; 3 is reached in every draw. `density`: diagonal entries of the diagonal blocks lie between 0.05 and 0.95, all other entries are small.
All inputs are finite; a program needn't handle non-finite values.
Results may differ from a plain program's by a relative error of at most 0.00013.
Values sent between devices are 32-bit elements; how exact they have to be, the bound alone decides.
No kernel may reach another device: no remote copies, remote signals or barrier semaphores. Data moves between devices by JAX's collectives and lax.ppermute only.
A program may use at most 64 MiB of HBM per device.

v0:
```python
import jax
import jax.numpy as jnp
from jax import lax
from jax.sharding import PartitionSpec as P

W = 3


def send(cells, shift):
    count = lax.axis_size("blk")
    return lax.ppermute(cells, "blk", [(i, (i + shift) % count) for i in range(count)])


def halo_pieces(cells):
    rows = cells.shape[0]
    tail = [cells[rows - W + k, W - k :] for k in range(W)]
    head = [cells[k, : 2 * W - k] for k in range(W)]
    return (tail, head)


def extend(right):
    tail, head = halo_pieces(right)
    from_left = send(jnp.concatenate(tail, axis=0), 1)
    from_right = send(jnp.concatenate(head, axis=0), -1)
    zero = jnp.zeros((1,) + right.shape[2:], right.dtype)
    rows = []
    start = 0
    for k in range(W):
        width = 2 * W + 1 - (W - k)
        piece = from_left[start : start + width]
        start += width
        rows.append(
            jnp.concatenate([jnp.broadcast_to(zero, (W - k,) + right.shape[2:]), piece], axis=0)
        )
    left = jnp.stack(rows)
    rows = []
    start = 0
    for k in range(W):
        width = 2 * W - k
        piece = from_right[start : start + width]
        start += width
        rows.append(
            jnp.concatenate([piece, jnp.broadcast_to(zero, (k + 1,) + right.shape[2:])], axis=0)
        )
    right_rows = jnp.stack(rows)
    return jnp.concatenate([left, right, right_rows], axis=0)


def contract(extended, shard_rows, keep=None):
    local_rows = shard_rows.shape[0]
    span = 2 * W + 1
    zeros = jnp.zeros_like(extended[:local_rows, :1])
    shifted = []
    for inner_band in range(span):
        window = extended[inner_band : inner_band + local_rows]
        shift = inner_band - W
        if shift > 0:
            window = jnp.concatenate([zeros] * shift + [window[:, : span - shift]], axis=1)
        elif shift < 0:
            window = jnp.concatenate([window[:, -shift:]] + [zeros] * -shift, axis=1)
        shifted.append(window)
    stacked = jnp.stack(shifted, axis=3)
    if keep is not None:
        shard_rows = shard_rows * keep
    return jnp.einsum("ibcas,iasr->ibcr", stacked, shard_rows, precision=lax.Precision.HIGH)


def on_device(density, band_widths):
    offsets = jnp.abs(jnp.arange(2 * W + 1, dtype=jnp.int32) - W)
    pattern = (offsets[None, :] <= band_widths[:, None]).astype(jnp.float32)[:, :, None, None]
    current = density * pattern
    for purify_step in range(2):
        if purify_step == 0:
            gathered, keep = (lax.all_gather(density, "col", axis=2, tiled=True), pattern)
        else:
            gathered, keep = (lax.all_gather(current, "col", axis=2, tiled=True), None)
        square = contract(extend(current), gathered, keep) * pattern
        third_power = contract(extend(square), gathered, keep) * pattern
        current = 3.0 * square - 2.0 * third_power
    return current


def solution(mesh):
    in_specs = (P("blk", None, "col", None), P("blk"))
    out_specs = P("blk", None, "col", None)
    return jax.shard_map(
        on_device, mesh=mesh, in_specs=in_specs, out_specs=out_specs, check_vma=False
    )
```

profile of v0, /device:TPU:97, one launch (start us, length us, event | category | flops | bytes accessed | tf_op | source)
XLA Modules:
  0.0 198.5 jit_solution(10707903417032842990)
XLA Ops:
  6.5 0.0 all-gather.3.cloned.1.call-start
  6.5 0.7 all-gather.3.cloned.1.call-update
  7.3 0.0 all-gather.5.cloned.1.call-start
  7.3 0.7 compare_convert_fusion
  8.0 1.1 broadcast_multiply_fusion
  9.2 0.0 copy-start.2
  9.2 3.4 %collective-permute-start = (f32[15,16,256]{2,1,0:T(8,128)S(1)}, f32[15,16,256]{2,1,0:T(8,128)S(1)}, u32[]{:S(2)}, u32[]{:S(2)}) collective-permute-start(f32[15,16,256]{2,1,0:T(8,128)S(1)} %pad_maximum_fusion), channel_id=1, source_target_pairs={{0,16},{16,32},{32,48},{48,64},{64,80},{80,96},{96,112},{112,128},... | collective-permute-start | bytes 737288 | tf_op jit(solution)/shard_map/ppermute | solution.py:11
  12.7 0.0 collective-permute-start.1
  12.7 3.1 %collective-permute-done = f32[15,16,256]{2,1,0:T(8,128)S(1)} collective-permute-done((f32[15,16,256]{2,1,0:T(8,128)S(1)}, f32[15,16,256]{2,1,0:T(8,128)S(1)}, u32[]{:S(2)}, u32[]{:S(2)}) %collective-permute-start) | collective-permute-done | bytes 245792 | tf_op jit(solution)/shard_map/ppermute | solution.py:11
  15.8 3.7 %collective-permute-done.1 = f32[15,16,256]{2,1,0:T(8,128)S(1)} collective-permute-done((f32[15,16,256]{2,1,0:T(8,128)S(1)}, f32[15,16,256]{2,1,0:T(8,128)S(1)}, u32[]{:S(2)}, u32[]{:S(2)}) %collective-permute-start.1) | collective-permute-done | bytes 245792 | tf_op jit(solution)/shard_map/ppermute | solution.py:11
  19.7 0.0 copy-done.2
  19.7 0.1 fusion.84
  19.8 0.0 copy-done.1
  19.8 0.1 bitcast_dynamic-update-slice_fusion
  20.0 66.8 %all-gather.3.cloned.1.call-done = f32[3,7,256,256]{3,2,1,0:T(8,128)} async-done(((f32[3,7,16,256]{3,2,1,0:T(8,128)}), f32[3,7,256,256]{3,2,1,0:T(8,128)}) %all-gather.3.cloned.1.call-update) | async-done | bytes 5505040 | tf_op jit(solution)/shard_map/all_gather | solution.py:74
  86.8 4.4 %fusion.16 = f32[3,7,16,256]{3,2,1,0:T(8,128)S(1)} fusion(f32[3,7,16,7,256]{4,2,3,1,0:T(8,128)S(1)} %fusion.68, f32[3,7,256,256]{3,2,1,0:T(8,128)} %all-gather.3.cloned.1.call-done, f32[3,7]{1,0:T(4,128)S(1)} %compare_convert_fusion), kind=kOutput, calls=%fused_computation.15 | convolution fusion | flops 926306304 | bytes 8257620 | tf_op jit(solution)/shard_map/ibcas,iasr->ibcr/dot_general | solution.py:65
  91.2 0.0 slice-start.1
  91.3 3.1 %collective-permute-start.2 = (f32[15,16,256]{2,1,0:T(8,128)S(1)}, f32[15,16,256]{2,1,0:T(8,128)S(1)}, u32[]{:S(2)}, u32[]{:S(2)}) collective-permute-start(f32[15,16,256]{2,1,0:T(8,128)S(1)} %pad_maximum_fusion.2), channel_id=1, source_target_pairs={{0,16},{16,32},{32,48},{48,64},{64,80},{80,96},{96,112},{112,128},... | collective-permute-start | bytes 737288 | tf_op jit(solution)/shard_map/ppermute | solution.py:11
  94.4 0.0 collective-permute-start.3
  94.4 3.1 %collective-permute-done.2 = f32[15,16,256]{2,1,0:T(8,128)S(1)} collective-permute-done((f32[15,16,256]{2,1,0:T(8,128)S(1)}, f32[15,16,256]{2,1,0:T(8,128)S(1)}, u32[]{:S(2)}, u32[]{:S(2)}) %collective-permute-start.2) | collective-permute-done | bytes 245792 | tf_op jit(solution)/shard_map/ppermute | solution.py:11
  97.7 3.5 %collective-permute-done.3 = f32[15,16,256]{2,1,0:T(8,128)S(1)} collective-permute-done((f32[15,16,256]{2,1,0:T(8,128)S(1)}, f32[15,16,256]{2,1,0:T(8,128)S(1)}, u32[]{:S(2)}, u32[]{:S(2)}) %collective-permute-start.3) | collective-permute-done | bytes 245792 | tf_op jit(solution)/shard_map/ppermute | solution.py:11
  101.3 0.1 fusion.83
  101.4 0.0 slice-done
  101.5 0.0 slice-done.1
  101.5 1.7 fusion.2
  103.2 0.8 fusion.80
  104.0 0.0 all-gather.5.cloned.1.call-update
  104.0 0.9 slice_bitcast_fusion.18
  105.0 1.0 slice_bitcast_fusion.10
  106.0 1.0 slice_bitcast_fusion.2
  106.9 0.2 collective-permute-start.4
  107.2 0.3 collective-permute-start.5
  107.5 2.8 %collective-permute-done.4 = f32[15,16,256]{2,1,0:T(8,128)S(1)} collective-permute-done((f32[15,16,256]{2,1,0:T(8,128)S(1)}, f32[15,16,256]{2,1,0:T(8,128)S(1)}, u32[]{:S(2)}, u32[]{:S(2)}) %collective-permute-start.4) | collective-permute-done | bytes 245792 | tf_op jit(solution)/shard_map/ppermute | solution.py:11
  110.3 3.7 %collective-permute-done.5 = f32[15,16,256]{2,1,0:T(8,128)S(1)} collective-permute-done((f32[15,16,256]{2,1,0:T(8,128)S(1)}, f32[15,16,256]{2,1,0:T(8,128)S(1)}, u32[]{:S(2)}, u32[]{:S(2)}) %collective-permute-start.5) | collective-permute-done | bytes 245792 | tf_op jit(solution)/shard_map/ppermute | solution.py:11
  114.2 0.0 copy-done
  114.2 0.1 fusion.82
  114.4 59.8 %all-gather.5.cloned.1.call-done = f32[3,7,256,256]{3,2,1,0:T(8,128)} async-done(((f32[3,7,16,256]{3,2,1,0:T(8,128)}), f32[3,7,256,256]{3,2,1,0:T(8,128)}) %all-gather.5.cloned.1.call-update) | async-done | bytes 5505040 | tf_op jit(solution)/shard_map/all_gather | solution.py:76
  174.2 4.4 %fusion.6 = f32[3,7,16,256,1]{3,2,0,1,4:T(8,128)S(1)} fusion(f32[3,7,16,7,256]{4,2,1,0,3:T(8,128)S(1)} %fusion.32, f32[3,7,256,256]{3,2,1,0:T(8,128)} %all-gather.5.cloned.1.call-done), kind=kOutput, calls=%fused_computation.6 | convolution fusion | flops 924844032 | bytes 8257536 | tf_op jit(solution)/shard_map/ibcas,iasr->ibcr/dot_general | solution.py:65
  178.7 0.1 bitcast_multiply_fusion.1
  178.8 0.0 slice-start.3
  178.9 3.1 %collective-permute-start.6 = (f32[15,16,256]{2,1,0:T(8,128)S(1)}, f32[15,16,256]{2,1,0:T(8,128)S(1)}, u32[]{:S(2)}, u32[]{:S(2)}) collective-permute-start(f32[15,16,256]{2,1,0:T(8,128)S(1)} %pad_maximum_fusion.6), channel_id=1, source_target_pairs={{0,16},{16,32},{32,48},{48,64},{64,80},{80,96},{96,112},{112,128},... | collective-permute-start | bytes 737288 | tf_op jit(solution)/shard_map/ppermute | solution.py:11
  181.9 0.0 collective-permute-start.7
  182.0 3.1 %collective-permute-done.6 = f32[15,16,256]{2,1,0:T(8,128)S(1)} collective-permute-done((f32[15,16,256]{2,1,0:T(8,128)S(1)}, f32[15,16,256]{2,1,0:T(8,128)S(1)}, u32[]{:S(2)}, u32[]{:S(2)}) %collective-permute-start.6) | collective-permute-done | bytes 245792 | tf_op jit(solution)/shard_map/ppermute | solution.py:11
  185.2 0.1 bitcast_dynamic-update-slice_fusion.1
  185.3 3.4 %collective-permute-done.7 = f32[15,16,256]{2,1,0:T(8,128)S(1)} collective-permute-done((f32[15,16,256]{2,1,0:T(8,128)S(1)}, f32[15,16,256]{2,1,0:T(8,128)S(1)}, u32[]{:S(2)}, u32[]{:S(2)}) %collective-permute-start.7) | collective-permute-done | bytes 245792 | tf_op jit(solution)/shard_map/ppermute | solution.py:11
  188.8 0.1 fusion.81
  189.0 1.8 fusion.4
  190.8 0.9 fusion.78
  (90 shorter events, 1.2 us)
Async XLA Ops:
  6.5 80.2 %all-gather.3.cloned.1.call-start = ((), (), s32[]{:S(2)}) async-start(), calls=%async_computation | async-start | bytes 5849088 | tf_op jit(solution)/shard_map/all_gather | solution.py:74
  7.3 167.0 %all-gather.5.cloned.1.call-start = ((), (), s32[]{:S(2)}) async-start(), calls=%async_computation.1 | async-start | bytes 5849088 | tf_op jit(solution)/shard_map/all_gather | solution.py:76
  9.2 10.5 %copy-start.2 = (pred[7]{0:T(512)(128)(4,1)S(1)}, pred[7]{0:T(512)(128)(4,1)}, u32[]{:S(2)}) copy-start(pred[7]{0:T(512)(128)(4,1)} %constant.7.clone.1) | copy-start | bytes 25
  9.2 6.6 %collective-permute-start = (f32[15,16,256]{2,1,0:T(8,128)S(1)}, f32[15,16,256]{2,1,0:T(8,128)S(1)}, u32[]{:S(2)}, u32[]{:S(2)}) collective-permute-start(f32[15,16,256]{2,1,0:T(8,128)S(1)} %pad_maximum_fusion), channel_id=1, source_target_pairs={{0,16},{16,32},{32,48},{48,64},{64,80},{80,96},{96,112},{112,128},... | collective-permute-start | bytes 737288 | tf_op jit(solution)/shard_map/ppermute | solution.py:11
  12.6 7.1 %copy-start.1 = (f32[3,7,16,256]{3,2,1,0:T(8,128)S(1)}, f32[3,7,16,256]{3,2,1,0:T(8,128)}, u32[]{:S(2)}) copy-start(f32[3,7,16,256]{3,2,1,0:T(8,128)} %param.2) | copy-start | bytes 1032196
  12.7 6.8 %collective-permute-start.1 = (f32[15,16,256]{2,1,0:T(8,128)S(1)}, f32[15,16,256]{2,1,0:T(8,128)S(1)}, u32[]{:S(2)}, u32[]{:S(2)}) collective-permute-start(f32[15,16,256]{2,1,0:T(8,128)S(1)} %pad_maximum_fusion.1), channel_id=1, source_target_pairs={{0,496},{16,0},{32,16},{48,32},{64,48},{80,64},{96,80},{112,96},{1... | collective-permute-start | bytes 737288 | tf_op jit(solution)/shard_map/ppermute | solution.py:11
  86.8 14.7 %slice-start = ((s8[5505024]{0:T(1024)(128)(4,1)}), s8[4194304]{0:T(1024)(128)(4,1)S(1)}, s32[]{:S(2)}) async-start(s8[5505024]{0:T(1024)(128)(4,1)} %bitcast.255), calls=%async_computation.2 | async-start | bytes 8388608
  91.2 10.2 %slice-start.1 = ((s8[5505024]{0:T(1024)(128)(4,1)}), s8[1310720]{0:T(1024)(128)(4,1)S(1)}, s32[]{:S(2)}) async-start(s8[5505024]{0:T(1024)(128)(4,1)} %bitcast.255), calls=%async_computation.3 | async-start | bytes 2621440
  91.3 6.2 %collective-permute-start.2 = (f32[15,16,256]{2,1,0:T(8,128)S(1)}, f32[15,16,256]{2,1,0:T(8,128)S(1)}, u32[]{:S(2)}, u32[]{:S(2)}) collective-permute-start(f32[15,16,256]{2,1,0:T(8,128)S(1)} %pad_maximum_fusion.2), channel_id=1, source_target_pairs={{0,16},{16,32},{32,48},{48,64},{64,80},{80,96},{96,112},{112,128},... | collective-permute-start | bytes 737288 | tf_op jit(solution)/shard_map/ppermute | solution.py:11
  94.4 6.8 %collective-permute-start.3 = (f32[15,16,256]{2,1,0:T(8,128)S(1)}, f32[15,16,256]{2,1,0:T(8,128)S(1)}, u32[]{:S(2)}, u32[]{:S(2)}) collective-permute-start(f32[15,16,256]{2,1,0:T(8,128)S(1)} %pad_maximum_fusion.3), channel_id=1, source_target_pairs={{0,496},{16,0},{32,16},{48,32},{64,48},{80,64},{96,80},{112,96},{1... | collective-permute-start | bytes 737288 | tf_op jit(solution)/shard_map/ppermute | solution.py:11
  104.0 10.1 %copy-start = (f32[3,7,16,256]{3,2,1,0:T(8,128)S(1)}, f32[3,7,16,256]{3,2,1,0:T(8,128)}, u32[]{:S(2)}) copy-start(f32[3,7,16,256]{3,2,1,0:T(8,128)} %fusion.80) | copy-start | bytes 1032196
  106.9 3.4 %collective-permute-start.4 = (f32[15,16,256]{2,1,0:T(8,128)S(1)}, f32[15,16,256]{2,1,0:T(8,128)S(1)}, u32[]{:S(2)}, u32[]{:S(2)}) collective-permute-start(f32[15,16,256]{2,1,0:T(8,128)S(1)} %pad_maximum_fusion.4), channel_id=1, source_target_pairs={{0,16},{16,32},{32,48},{48,64},{64,80},{80,96},{96,112},{112,128},... | collective-permute-start | bytes 737288 | tf_op jit(solution)/shard_map/ppermute | solution.py:11
  107.2 6.8 %collective-permute-start.5 = (f32[15,16,256]{2,1,0:T(8,128)S(1)}, f32[15,16,256]{2,1,0:T(8,128)S(1)}, u32[]{:S(2)}, u32[]{:S(2)}) collective-permute-start(f32[15,16,256]{2,1,0:T(8,128)S(1)} %pad_maximum_fusion.5), channel_id=1, source_target_pairs={{0,496},{16,0},{32,16},{48,32},{64,48},{80,64},{96,80},{112,96},{1... | collective-permute-start | bytes 737288 | tf_op jit(solution)/shard_map/ppermute | solution.py:11
  174.2 14.8 %slice-start.2 = ((s8[5505024]{0:T(1024)(128)(4,1)}), s8[4194304]{0:T(1024)(128)(4,1)S(1)}, s32[]{:S(2)}) async-start(s8[5505024]{0:T(1024)(128)(4,1)} %bitcast.257), calls=%async_computation.4 | async-start | bytes 8388608
  178.8 10.3 %slice-start.3 = ((s8[5505024]{0:T(1024)(128)(4,1)}), s8[1310720]{0:T(1024)(128)(4,1)S(1)}, s32[]{:S(2)}) async-start(s8[5505024]{0:T(1024)(128)(4,1)} %bitcast.257), calls=%async_computation.5 | async-start | bytes 2621440
  178.9 6.2 %collective-permute-start.6 = (f32[15,16,256]{2,1,0:T(8,128)S(1)}, f32[15,16,256]{2,1,0:T(8,128)S(1)}, u32[]{:S(2)}, u32[]{:S(2)}) collective-permute-start(f32[15,16,256]{2,1,0:T(8,128)S(1)} %pad_maximum_fusion.6), channel_id=1, source_target_pairs={{0,16},{16,32},{32,48},{48,64},{64,80},{80,96},{96,112},{112,128},... | collective-permute-start | bytes 737288 | tf_op jit(solution)/shard_map/ppermute | solution.py:11
  181.9 6.8 %collective-permute-start.7 = (f32[15,16,256]{2,1,0:T(8,128)S(1)}, f32[15,16,256]{2,1,0:T(8,128)S(1)}, u32[]{:S(2)}, u32[]{:S(2)}) collective-permute-start(f32[15,16,256]{2,1,0:T(8,128)S(1)} %pad_maximum_fusion.7), channel_id=1, source_target_pairs={{0,496},{16,0},{32,16},{48,32},{64,48},{80,64},{96,80},{112,96},{1... | collective-permute-start | bytes 737288 | tf_op jit(solution)/shard_map/ppermute | solution.py:11
Sparse Core Ops, SparseCore 0:
  10.4 76.3 all-gather.2
  104.2 70.0 all-gather.4
where the time goes:
time: 199 us; the launch traced here: 198 us
  waiting for transfers between devices  154 us (77%)
  between operations  14.1 us (7%)
  matrix products  12.3 us (6%)
  starting transfers between devices  10.2 us (5%)
  other arithmetic  4.81 us (2%)
  local copies, waits for them, and re-layouts  3.36 us (2%)
    all_gather x1, waiting for transfers between devices, on_device(): lax.all_gather(density, 'col', axis=2, tiled=True)  66.8 us
    all_gather x1, waiting for transfers between devices, on_device(): gathered, keep = (lax.all_gather(current, 'col', axis=2, tiled=True), None)  59.8 us
    ppermute x8, waiting for transfers between devices, send(): lax.ppermute(cells, 'blk', [(i, (i + shift) % count) for i in range(count)])  26.4 us
    dot_general x4, matrix products, contract(): jnp.einsum('ibcas,iasr->ibcr', stacked, shard_rows, precision=lax.Precisi...  12.3 us
    ppermute x8, starting transfers between devices, send(): lax.ppermute(cells, 'blk', [(i, (i + shift) % count) for i in range(count)])  10.1 us
  transfers between devices with their start and end apart: 10, of which 10 were waited for; matrix products, arithmetic and copies ran while one was open for 3% of the time, Pallas kernels for 0%

commit v1 on v0

--- a/solution.py
+++ b/solution.py
@@ -71,7 +71,12 @@
     current = density * pattern
     for purify_step in range(2):
         if purify_step == 0:
-            gathered, keep = (lax.all_gather(density, "col", axis=2, tiled=True), pattern)
+            gathered, keep = (
+                jnp.concatenate(
+                    lax.all_to_all(jnp.stack([density] * lax.axis_size("col")), "col", 0, 0), axis=2
+                ),
+                pattern,
+            )
         else:
             gathered, keep = (lax.all_gather(current, "col", axis=2, tiled=True), None)
         square = contract(extend(current), gathered, keep) * pattern

time: 199 us -> 216 us (1.085)
  starting transfers between devices: 10.2 us -> 18.9 us
  local copies, waits for them, and re-layouts: 3.36 us -> 10.7 us
  waiting for transfers between devices: 154 us -> 158 us
    all_to_all x0 -> x1, waiting for transfers between devices: none -> 69.3 us  [on_device(): lax.all_to_all(jnp.stack([density] * lax.axis_size('col')), 'col', 0, 0)]
    all_gather x1 -> x0, waiting for transfers between devices: 66.8 us -> none  [on_device(): lax.all_gather(density, 'col', axis=2, tiled=True)]
    all_to_all x0 -> x1, starting transfers between devices: none -> 6.93 us  [on_device(): lax.all_to_all(jnp.stack([density] * lax.axis_size('col')), 'col', 0, 0)]
    another operation x0 -> x1, local copies, waits for them, and re-layouts: none -> 4.16 us  [on_device(): jnp.stack([density] * lax.axis_size('col'))]
    all_to_all x0 -> x1, local copies, waits for them, and re-layouts: none -> 3.18 us  [on_device(): lax.all_to_all(jnp.stack([density] * lax.axis_size('col')), 'col', 0, 0)]
  transfers between devices with their start and end apart: 10 -> 10, of which waited for: 10 -> 10; matrix products, arithmetic and copies ran while one was open for 3% -> 2% of each run, Pallas kernels for 0% -> 0%
where the time goes in v1:
time: 216 us
  waiting for transfers between devices  158 us (73%)
  starting transfers between devices  18.9 us (9%)
  between operations  14.1 us (7%)
  local copies, waits for them, and re-layouts  10.7 us (5%)
  matrix products  10.3 us (5%)
  other arithmetic  4.15 us (2%)
    all_to_all x1, waiting for transfers between devices, on_device(): lax.all_to_all(jnp.stack([density] * lax.axis_size('col')), 'col', 0, 0)  69.3 us
    all_gather x1, waiting for transfers between devices, on_device(): gathered, keep = (lax.all_gather(current, 'col', axis=2, tiled=True), None)  61.6 us
    ppermute x8, waiting for transfers between devices, send(): lax.ppermute(cells, 'blk', [(i, (i + shift) % count) for i in range(count)])  27 us
    ppermute x8, starting transfers between devices, send(): lax.ppermute(cells, 'blk', [(i, (i + shift) % count) for i in range(count)])  11.9 us
    dot_general x4, matrix products, contract(): jnp.einsum('ibcas,iasr->ibcr', stacked, shard_rows, precision=lax.Precisi...  10.3 us
    all_to_all x1, starting transfers between devices, on_device(): lax.all_to_all(jnp.stack([density] * lax.axis_size('col')), 'col', 0, 0)  6.93 us
  transfers between devices with their start and end apart: 10, of which 10 were waited for; matrix products, arithmetic and copies ran while one was open for 2% of the time, Pallas kernels for 0%

profile of v1, /device:TPU:97, one launch (start us, length us, event | category | flops | bytes accessed | tf_op | source)
XLA Modules:
  0.0 216.1 jit_solution(17828560438047684979)
XLA Ops:
  6.5 4.2 %stack.227 = f32[16,3,7,16,256]{4,3,2,1,0:T(8,128)} broadcast(f32[3,7,16,256]{3,2,1,0:T(8,128)} %param.2), dimensions={1,2,3,4} | broadcast | bytes 5849088 | tf_op jit(solution)/shard_map/stack | solution.py:76
  10.7 6.9 %all-to-all-start = ((f32[16,3,7,16,256]{4,3,2,1,0:T(8,128)}), f32[16,3,7,16,256]{4,3,2,1,0:T(8,128)}, u32[]{:S(2)}, u32[]{:S(2)}) async-start(f32[16,3,7,16,256]{4,3,2,1,0:T(8,128)} %stack.227), calls=%async_computation | async-start | bytes 11010048 | tf_op jit(solution)/shard_map/all_to_all | solution.py:76
  17.6 0.0 all-gather.2.cloned.1.call-start
  17.7 0.0 copy-done.3
  17.7 0.1 compare_convert_fusion
  17.8 0.0 copy-done.1
  17.8 0.1 broadcast_multiply_fusion
  17.9 0.0 copy-start.2
  18.0 3.7 %collective-permute-start = (f32[15,16,256]{2,1,0:T(8,128)S(1)}, f32[15,16,256]{2,1,0:T(8,128)S(1)}, u32[]{:S(2)}, u32[]{:S(2)}) collective-permute-start(f32[15,16,256]{2,1,0:T(8,128)S(1)} %pad_maximum_fusion), channel_id=1, source_target_pairs={{0,16},{16,32},{32,48},{48,64},{64,80},{80,96},{96,112},{112,128},... | collective-permute-start | bytes 737288 | tf_op jit(solution)/shard_map/ppermute | solution.py:11
  21.7 0.0 collective-permute-start.1
  21.7 3.1 %collective-permute-done = f32[15,16,256]{2,1,0:T(8,128)S(1)} collective-permute-done((f32[15,16,256]{2,1,0:T(8,128)S(1)}, f32[15,16,256]{2,1,0:T(8,128)S(1)}, u32[]{:S(2)}, u32[]{:S(2)}) %collective-permute-start) | collective-permute-done | bytes 245792 | tf_op jit(solution)/shard_map/ppermute | solution.py:11
  24.9 4.1 %collective-permute-done.1 = f32[15,16,256]{2,1,0:T(8,128)S(1)} collective-permute-done((f32[15,16,256]{2,1,0:T(8,128)S(1)}, f32[15,16,256]{2,1,0:T(8,128)S(1)}, u32[]{:S(2)}, u32[]{:S(2)}) %collective-permute-start.1) | collective-permute-done | bytes 245792 | tf_op jit(solution)/shard_map/ppermute | solution.py:11
  29.1 0.0 copy-done.2
  29.1 0.1 fusion.97
  29.2 0.1 bitcast_dynamic-update-slice_fusion
  29.4 69.3 %all-to-all-done = f32[16,3,7,16,256]{4,3,2,1,0:T(8,128)} async-done(((f32[16,3,7,16,256]{4,3,2,1,0:T(8,128)}), f32[16,3,7,16,256]{4,3,2,1,0:T(8,128)}, u32[]{:S(2)}, u32[]{:S(2)}) %all-to-all-start) | async-done | bytes 5505056 | tf_op jit(solution)/shard_map/all_to_all | solution.py:76
  98.7 3.2 %copy.27 = f32[16,3,7,16,256]{4,3,0,2,1:T(8,128)S(1)} copy(f32[16,3,7,16,256]{4,3,2,1,0:T(8,128)} %all-to-all-done) | data formatting | bytes 11010048 | tf_op jit(solution)/shard_map/all_to_all | solution.py:76
  101.9 1.0 bitcast_multiply_fusion
  102.9 2.1 fusion.29
  105.1 4.6 %collective-permute-start.2 = (f32[15,16,256]{2,1,0:T(8,128)S(1)}, f32[15,16,256]{2,1,0:T(8,128)S(1)}, u32[]{:S(2)}, u32[]{:S(2)}) collective-permute-start(f32[15,16,256]{2,1,0:T(8,128)S(1)} %pad_maximum_fusion.2), channel_id=1, source_target_pairs={{0,16},{16,32},{32,48},{48,64},{64,80},{80,96},{96,112},{112,128},... | collective-permute-start | bytes 737288 | tf_op jit(solution)/shard_map/ppermute | solution.py:11
  109.7 0.0 collective-permute-start.3
  109.7 3.1 %collective-permute-done.2 = f32[15,16,256]{2,1,0:T(8,128)S(1)} collective-permute-done((f32[15,16,256]{2,1,0:T(8,128)S(1)}, f32[15,16,256]{2,1,0:T(8,128)S(1)}, u32[]{:S(2)}, u32[]{:S(2)}) %collective-permute-start.2) | collective-permute-done | bytes 245792 | tf_op jit(solution)/shard_map/ppermute | solution.py:11
  112.9 3.6 %collective-permute-done.3 = f32[15,16,256]{2,1,0:T(8,128)S(1)} collective-permute-done((f32[15,16,256]{2,1,0:T(8,128)S(1)}, f32[15,16,256]{2,1,0:T(8,128)S(1)}, u32[]{:S(2)}, u32[]{:S(2)}) %collective-permute-start.3) | collective-permute-done | bytes 245792 | tf_op jit(solution)/shard_map/ppermute | solution.py:11
  116.7 0.1 fusion.96
  116.9 2.1 fusion.21
  118.9 0.8 fusion.93
  119.8 0.0 all-gather.2.cloned.1.call-update
  119.8 0.9 slice_bitcast_fusion.18
  120.7 1.0 slice_bitcast_fusion.10
  121.7 1.0 slice_bitcast_fusion.2
  122.7 0.1 collective-permute-start.4
  122.8 0.4 collective-permute-start.5
  123.3 2.7 %collective-permute-done.4 = f32[15,16,256]{2,1,0:T(8,128)S(1)} collective-permute-done((f32[15,16,256]{2,1,0:T(8,128)S(1)}, f32[15,16,256]{2,1,0:T(8,128)S(1)}, u32[]{:S(2)}, u32[]{:S(2)}) %collective-permute-start.4) | collective-permute-done | bytes 245792 | tf_op jit(solution)/shard_map/ppermute | solution.py:11
  126.0 3.7 %collective-permute-done.5 = f32[15,16,256]{2,1,0:T(8,128)S(1)} collective-permute-done((f32[15,16,256]{2,1,0:T(8,128)S(1)}, f32[15,16,256]{2,1,0:T(8,128)S(1)}, u32[]{:S(2)}, u32[]{:S(2)}) %collective-permute-start.5) | collective-permute-done | bytes 245792 | tf_op jit(solution)/shard_map/ppermute | solution.py:11
  129.8 0.0 copy-done
  129.9 0.1 fusion.95
  130.1 61.6 %all-gather.2.cloned.1.call-done = f32[3,7,256,256]{3,2,1,0:T(8,128)} async-done(((f32[3,7,16,256]{3,2,1,0:T(8,128)}), f32[3,7,256,256]{3,2,1,0:T(8,128)}) %all-gather.2.cloned.1.call-update) | async-done | bytes 5505040 | tf_op jit(solution)/shard_map/all_gather | solution.py:81
  191.6 4.4 %fusion.11 = f32[3,7,16,256]{3,2,0,1:T(8,128)S(1)} fusion(f32[3,7,16,7,256]{4,2,1,0,3:T(8,128)S(1)} %fusion.45, f32[3,7,256,256]{3,2,1,0:T(8,128)} %all-gather.2.cloned.1.call-done), kind=kOutput, calls=%fused_computation.12 | convolution fusion | flops 924844032 | bytes 8257536 | tf_op jit(solution)/shard_map/ibcas,iasr->ibcr/dot_general | solution.py:65
  196.1 0.1 copy_multiply_fusion.1
  196.2 0.0 slice-start.1
  196.3 3.1 %collective-permute-start.6 = (f32[15,16,256]{2,1,0:T(8,128)S(1)}, f32[15,16,256]{2,1,0:T(8,128)S(1)}, u32[]{:S(2)}, u32[]{:S(2)}) collective-permute-start(f32[15,16,256]{2,1,0:T(8,128)S(1)} %pad_maximum_fusion.6), channel_id=1, source_target_pairs={{0,16},{16,32},{32,48},{48,64},{64,80},{80,96},{96,112},{112,128},... | collective-permute-start | bytes 737288 | tf_op jit(solution)/shard_map/ppermute | solution.py:11
  199.3 0.0 collective-permute-start.7
  199.4 3.1 %collective-permute-done.6 = f32[15,16,256]{2,1,0:T(8,128)S(1)} collective-permute-done((f32[15,16,256]{2,1,0:T(8,128)S(1)}, f32[15,16,256]{2,1,0:T(8,128)S(1)}, u32[]{:S(2)}, u32[]{:S(2)}) %collective-permute-start.6) | collective-permute-done | bytes 245792 | tf_op jit(solution)/shard_map/ppermute | solution.py:11
  202.5 3.6 %collective-permute-done.7 = f32[15,16,256]{2,1,0:T(8,128)S(1)} collective-permute-done((f32[15,16,256]{2,1,0:T(8,128)S(1)}, f32[15,16,256]{2,1,0:T(8,128)S(1)}, u32[]{:S(2)}, u32[]{:S(2)}) %collective-permute-start.7) | collective-permute-done | bytes 245792 | tf_op jit(solution)/shard_map/ppermute | solution.py:11
  206.3 0.1 bitcast_dynamic-update-slice_fusion.1
  206.4 0.1 fusion.94
  206.6 1.8 fusion.16
  208.4 0.9 fusion.91
  (89 shorter events, 1.2 us)
Async XLA Ops:
  10.7 7.0 %copy-start.3 = (s32[3]{0:T(128)S(1)}, s32[3]{0:T(128)}, u32[]{:S(2)}) copy-start(s32[3]{0:T(128)} %param.3) | copy-start | bytes 40
  10.7 7.1 %copy-start.1 = (f32[3,7,16,256]{3,2,1,0:T(8,128)S(1)}, f32[3,7,16,256]{3,2,1,0:T(8,128)}, u32[]{:S(2)}) copy-start(f32[3,7,16,256]{3,2,1,0:T(8,128)} %param.2) | copy-start | bytes 1032196
  10.7 88.0 %all-to-all-start = ((f32[16,3,7,16,256]{4,3,2,1,0:T(8,128)}), f32[16,3,7,16,256]{4,3,2,1,0:T(8,128)}, u32[]{:S(2)}, u32[]{:S(2)}) async-start(f32[16,3,7,16,256]{4,3,2,1,0:T(8,128)} %stack.227), calls=%async_computation | async-start | bytes 11010048 | tf_op jit(solution)/shard_map/all_to_all | solution.py:76
  17.6 174.0 %all-gather.2.cloned.1.call-start = ((), (), s32[]{:S(2)}) async-start(), calls=%async_computation.1 | async-start | bytes 5849088 | tf_op jit(solution)/shard_map/all_gather | solution.py:81
  17.9 11.2 %copy-start.2 = (pred[7]{0:T(512)(128)(4,1)S(1)}, pred[7]{0:T(512)(128)(4,1)}, u32[]{:S(2)}) copy-start(pred[7]{0:T(512)(128)(4,1)} %constant.7.clone.1) | copy-start | bytes 25
  18.0 6.8 %collective-permute-start = (f32[15,16,256]{2,1,0:T(8,128)S(1)}, f32[15,16,256]{2,1,0:T(8,128)S(1)}, u32[]{:S(2)}, u32[]{:S(2)}) collective-permute-start(f32[15,16,256]{2,1,0:T(8,128)S(1)} %pad_maximum_fusion), channel_id=1, source_target_pairs={{0,16},{16,32},{32,48},{48,64},{64,80},{80,96},{96,112},{112,128},... | collective-permute-start | bytes 737288 | tf_op jit(solution)/shard_map/ppermute | solution.py:11
  21.7 7.2 %collective-permute-start.1 = (f32[15,16,256]{2,1,0:T(8,128)S(1)}, f32[15,16,256]{2,1,0:T(8,128)S(1)}, u32[]{:S(2)}, u32[]{:S(2)}) collective-permute-start(f32[15,16,256]{2,1,0:T(8,128)S(1)} %pad_maximum_fusion.1), channel_id=1, source_target_pairs={{0,496},{16,0},{32,16},{48,32},{64,48},{80,64},{96,80},{112,96},{1... | collective-permute-start | bytes 737288 | tf_op jit(solution)/shard_map/ppermute | solution.py:11
  105.1 7.7 %collective-permute-start.2 = (f32[15,16,256]{2,1,0:T(8,128)S(1)}, f32[15,16,256]{2,1,0:T(8,128)S(1)}, u32[]{:S(2)}, u32[]{:S(2)}) collective-permute-start(f32[15,16,256]{2,1,0:T(8,128)S(1)} %pad_maximum_fusion.2), channel_id=1, source_target_pairs={{0,16},{16,32},{32,48},{48,64},{64,80},{80,96},{96,112},{112,128},... | collective-permute-start | bytes 737288 | tf_op jit(solution)/shard_map/ppermute | solution.py:11
  109.7 6.8 %collective-permute-start.3 = (f32[15,16,256]{2,1,0:T(8,128)S(1)}, f32[15,16,256]{2,1,0:T(8,128)S(1)}, u32[]{:S(2)}, u32[]{:S(2)}) collective-permute-start(f32[15,16,256]{2,1,0:T(8,128)S(1)} %pad_maximum_fusion.3), channel_id=1, source_target_pairs={{0,496},{16,0},{32,16},{48,32},{64,48},{80,64},{96,80},{112,96},{1... | collective-permute-start | bytes 737288 | tf_op jit(solution)/shard_map/ppermute | solution.py:11
  119.8 10.0 %copy-start = (f32[3,7,16,256]{3,2,1,0:T(8,128)S(1)}, f32[3,7,16,256]{3,2,1,0:T(8,128)}, u32[]{:S(2)}) copy-start(f32[3,7,16,256]{3,2,1,0:T(8,128)} %fusion.93) | copy-start | bytes 1032196
  122.7 3.2 %collective-permute-start.4 = (f32[15,16,256]{2,1,0:T(8,128)S(1)}, f32[15,16,256]{2,1,0:T(8,128)S(1)}, u32[]{:S(2)}, u32[]{:S(2)}) collective-permute-start(f32[15,16,256]{2,1,0:T(8,128)S(1)} %pad_maximum_fusion.4), channel_id=1, source_target_pairs={{0,16},{16,32},{32,48},{48,64},{64,80},{80,96},{96,112},{112,128},... | collective-permute-start | bytes 737288 | tf_op jit(solution)/shard_map/ppermute | solution.py:11
  122.8 6.8 %collective-permute-start.5 = (f32[15,16,256]{2,1,0:T(8,128)S(1)}, f32[15,16,256]{2,1,0:T(8,128)S(1)}, u32[]{:S(2)}, u32[]{:S(2)}) collective-permute-start(f32[15,16,256]{2,1,0:T(8,128)S(1)} %pad_maximum_fusion.5), channel_id=1, source_target_pairs={{0,496},{16,0},{32,16},{48,32},{64,48},{80,64},{96,80},{112,96},{1... | collective-permute-start | bytes 737288 | tf_op jit(solution)/shard_map/ppermute | solution.py:11
  191.6 15.0 %slice-start = ((s8[5505024]{0:T(1024)(128)(4,1)}), s8[4194304]{0:T(1024)(128)(4,1)S(1)}, s32[]{:S(2)}) async-start(s8[5505024]{0:T(1024)(128)(4,1)} %bitcast.249), calls=%async_computation.2 | async-start | bytes 8388608
  196.2 10.5 %slice-start.1 = ((s8[5505024]{0:T(1024)(128)(4,1)}), s8[1310720]{0:T(1024)(128)(4,1)S(1)}, s32[]{:S(2)}) async-start(s8[5505024]{0:T(1024)(128)(4,1)} %bitcast.249), calls=%async_computation.3 | async-start | bytes 2621440
  196.3 6.2 %collective-permute-start.6 = (f32[15,16,256]{2,1,0:T(8,128)S(1)}, f32[15,16,256]{2,1,0:T(8,128)S(1)}, u32[]{:S(2)}, u32[]{:S(2)}) collective-permute-start(f32[15,16,256]{2,1,0:T(8,128)S(1)} %pad_maximum_fusion.6), channel_id=1, source_target_pairs={{0,16},{16,32},{32,48},{48,64},{64,80},{80,96},{96,112},{112,128},... | collective-permute-start | bytes 737288 | tf_op jit(solution)/shard_map/ppermute | solution.py:11
  199.3 6.8 %collective-permute-start.7 = (f32[15,16,256]{2,1,0:T(8,128)S(1)}, f32[15,16,256]{2,1,0:T(8,128)S(1)}, u32[]{:S(2)}, u32[]{:S(2)}) collective-permute-start(f32[15,16,256]{2,1,0:T(8,128)S(1)} %pad_maximum_fusion.7), channel_id=1, source_target_pairs={{0,496},{16,0},{32,16},{48,32},{64,48},{80,64},{96,80},{112,96},{1... | collective-permute-start | bytes 737288 | tf_op jit(solution)/shard_map/ppermute | solution.py:11
Sparse Core Ops, SparseCore 0:
  119.9 71.6 all-gather.1
